TPU v7x, 256 devices: a whole 4x4x8 slice. The times are simulated.
256 devices in a mesh: pipe: 4 (over x), seq: 64 (over z, y, core).
Axes of the slice: x: 4, y: 4, z: 8, core: 2. Of those that a mesh axis runs over, the one named last changes fastest.
Arguments:
- inputs: bfloat16 [4, 2, 8192, 1024], P('pipe', None, 'seq'), may hold values from -16 to 16
- incoming: bfloat16 [4, 2, 8192, 1024], P('pipe', None, 'seq'), may hold values from -6 to 6
- angles: float32 [4, 2, 1024], P('pipe'), may hold values from -3.140625 to 3.140625
- level_weights: float32 [4, 14, 1024], P('pipe'), may hold values from -1.5 to 1.5
- mix_weight: bfloat16 [4, 1024, 2048], P('pipe'), may hold values from -0.1875 to 0.1875
Outputs:
- grad_input: bfloat16 [4, 2, 8192, 1024], P('pipe', None, 'seq')
- grad_angles: float32 [4, 2, 1024], P('pipe')
- grad_levels: float32 [4, 14, 1024], P('pipe')
- grad_mix: float32 [4, 1024, 2048], P('pipe', 'seq')
All inputs are finite; a program needn't handle non-finite values.
Results may differ from a plain program's by a relative error of at most 0.015.
Values may be sent and summed in bfloat16 or wider, within the bound.
No kernel may reach another device: no remote copies, remote signals or barrier semaphores. Data moves between devices by JAX's collectives and lax.ppermute only.
A program may use at most 128 MiB of HBM per device.

v0:
```python
import jax
import jax.numpy as jnp
from jax import lax
from jax.sharding import PartitionSpec as P


def shifted_2(block, axis, distance):
    devices = range(lax.axis_size(axis))
    route = [(i - distance, i) for i in devices if i - distance in devices]
    return lax.ppermute(block, axis, route)


def shifted_3(value, axis, steps):
    count = lax.axis_size(axis)
    pairs = [(source, (source + steps) % count) for source in range(count)]
    return lax.ppermute(value, axis, pairs)


def rounded(values):
    return lax.optimization_barrier(values.astype(jnp.bfloat16))


def near_behind(state_now, spacing, positions):
    rim_rows = shifted_2(state_now[:, positions - spacing :, :], "seq", 1)
    return jnp.concatenate([rim_rows, state_now[:, : positions - spacing, :]], axis=1)


def tap_terms(totals, adjoint, weighted, current, previous):
    return (
        totals[0] + jnp.sum(adjoint * current, axis=(0, 1)),
        totals[1] + jnp.sum(adjoint * previous, axis=(0, 1)),
        totals[2] + jnp.sum(weighted * current, axis=(0, 1)),
        totals[3] + jnp.sum(weighted * previous, axis=(0, 1)),
    )


def shards(inputs, incoming, angles, level_weights, mix_weight):
    activations = inputs[0]
    sequences, positions, channels = activations.shape
    seq_devices = lax.axis_size("seq")
    levels = level_weights.shape[1] - 1
    near_count = positions.bit_length() - 1
    grad_scale = float(sequences * positions * seq_devices) ** (-0.5)
    weights = level_weights[0]
    w_mix = mix_weight[0]
    c_low = jnp.cos(angles[0, 0])
    s_low = jnp.sin(angles[0, 0])
    c_high = jnp.cos(angles[0, 1])
    s_high = jnp.sin(angles[0, 1])
    received = shifted_3(incoming, "pipe", -1)[0]
    states = []
    shifted_states = []
    mixed = jnp.zeros(activations.shape, jnp.float32)
    state_now = activations
    for level_idx in range(near_count):
        spacing = 2**level_idx
        shifted = near_behind(state_now, spacing, positions)
        current = state_now.astype(jnp.float32)
        previous = shifted.astype(jnp.float32)
        mixed = mixed + weights[level_idx] * (c_high * current + s_high * previous)
        states.append(state_now)
        shifted_states.append(shifted)
        state_now = rounded(c_low * current + s_low * previous)
    for level_idx in range(near_count, levels):
        spacing = 2**level_idx
        shifted = shifted_2(state_now, "seq", spacing // positions)
        current = state_now.astype(jnp.float32)
        previous = shifted.astype(jnp.float32)
        mixed = mixed + weights[level_idx] * (c_high * current + s_high * previous)
        states.append(state_now)
        shifted_states.append(shifted)
        state_now = rounded(c_low * current + s_low * previous)
    top_state = state_now.astype(jnp.float32)
    mixed = mixed + weights[levels] * top_state
    activated = jax.nn.gelu(mixed).astype(jnp.bfloat16).reshape(-1, channels)
    projected = jnp.dot(activated, w_mix, preferred_element_type=jnp.float32)
    value_half = projected[:, :channels]
    gate_value = jax.nn.sigmoid(projected[:, channels:])
    upstream = received.reshape(-1, channels).astype(jnp.float32)
    grad_proj = jnp.concatenate(
        [upstream * gate_value, upstream * value_half * gate_value * (1.0 - gate_value)], axis=1
    ).astype(jnp.bfloat16)
    grad_act = jnp.einsum("rk,ck->rc", grad_proj, w_mix, preferred_element_type=jnp.float32)
    grad_weight = (
        lax.psum_scatter(
            jnp.einsum("rc,rk->ck", activated, grad_proj, preferred_element_type=jnp.float32),
            "seq",
            scatter_dimension=0,
            tiled=True,
        )
        * grad_scale
    )
    _, pullback = jax.vjp(jax.nn.gelu, mixed)
    grad_conv = pullback(grad_act.reshape(mixed.shape))[0]
    level_grads = [None] * (levels + 1)
    adjoint = weights[levels] * grad_conv
    level_grads[levels] = jnp.sum(grad_conv * top_state, axis=(0, 1))
    zero_row = jnp.zeros((channels,), jnp.float32)
    totals = (zero_row, zero_row, zero_row, zero_row)
    for level_idx in reversed(range(near_count, levels)):
        spacing = 2**level_idx
        current = states[level_idx].astype(jnp.float32)
        previous = shifted_states[level_idx].astype(jnp.float32)
        weighted = weights[level_idx] * grad_conv
        level_grads[level_idx] = jnp.sum(
            grad_conv * (c_high * current + s_high * previous), axis=(0, 1)
        )
        totals = tap_terms(totals, adjoint, weighted, current, previous)
        carried = rounded(s_low * adjoint + s_high * weighted)
        arrived = shifted_2(carried, "seq", -(spacing // positions)).astype(jnp.float32)
        adjoint = c_low * adjoint + c_high * weighted + arrived
    for level_idx in reversed(range(near_count)):
        spacing = 2**level_idx
        current = states[level_idx].astype(jnp.float32)
        previous = shifted_states[level_idx].astype(jnp.float32)
        weighted = weights[level_idx] * grad_conv
        level_grads[level_idx] = jnp.sum(
            grad_conv * (c_high * current + s_high * previous), axis=(0, 1)
        )
        totals = tap_terms(totals, adjoint, weighted, current, previous)
        carried = rounded(s_low * adjoint + s_high * weighted)
        rim_rows = shifted_2(carried[:, :spacing, :], "seq", -1)
        arrived = jnp.concatenate([carried[:, spacing:, :], rim_rows], axis=1).astype(jnp.float32)
        adjoint = c_low * adjoint + c_high * weighted + arrived
    angle_terms = jnp.stack(
        [c_low * totals[1] - s_low * totals[0], c_high * totals[3] - s_high * totals[2]]
    )
    angle_total, level_total = lax.psum((angle_terms, jnp.stack(level_grads)), "seq")
    grad_input = (received.astype(jnp.float32) + adjoint).astype(jnp.bfloat16)
    return (
        grad_input[None],
        (angle_total * grad_scale)[None],
        (level_total * grad_scale)[None],
        grad_weight[None],
    )


def solution(mesh):
    placed = (
        P("pipe", None, "seq", None),
        P("pipe", None, "seq", None),
        P("pipe", None, None),
        P("pipe", None, None),
        P("pipe", None, None),
    )
    return jax.shard_map(
        shards,
        mesh=mesh,
        in_specs=placed,
        out_specs=(
            P("pipe", None, "seq", None),
            P("pipe", None, None),
            P("pipe", None, None),
            P("pipe", "seq", None),
        ),
        check_vma=False,
    )
```

profile of v0, /device:TPU:2, one launch (start us, length us, event | category | flops | bytes accessed | tf_op | source)
XLA Modules:
  0.0 706.3 jit_solution(15345391207127334861)
XLA Ops:
  8.0 1.7 collective-permute-start.1
  9.7 1.0 slice_cosine_fusion
  10.8 1.5 fusion.14
  12.3 3.8 collective-permute-start.2
  17.1 3.9 collective-permute-start.3
  22.2 4.2 collective-permute-start.4
  27.4 4.4 collective-permute-start.5
  32.9 4.7 collective-permute-start.6
  38.8 5.2 collective-permute-start.7
  44.1 1.1 collective-permute-done.7
  45.5 6.7 collective-permute-start.8
  52.1 1.5 collective-permute-done.8
  53.8 11.5 %collective-permute-start.9 = (bf16[2,128,1024]{2,1,0:T(8,128)(2,1)S(1)}, bf16[2,128,1024]{2,1,0:T(8,128)(2,1)S(1)}, u32[]{:S(2)}, u32[]{:S(2)}) collective-permute-start(bf16[2,128,1024]{2,1,0:T(8,128)(2,1)S(1)} %fusion.63), channel_id=1, source_target_pairs={{0,2},{1,3},{2,4},{3,5},{4,6},{5,7},{6,8},{7,9},{8,10},{9,11},{10,... | collective-permute-start | bytes 1572872 | tf_op jit(solution)/shard_map/ppermute | solution.py:10
  65.4 10.5 %collective-permute-done.9 = bf16[2,128,1024]{2,1,0:T(8,128)(2,1)S(1)} collective-permute-done((bf16[2,128,1024]{2,1,0:T(8,128)(2,1)S(1)}, bf16[2,128,1024]{2,1,0:T(8,128)(2,1)S(1)}, u32[]{:S(2)}, u32[]{:S(2)}) %collective-permute-start.9) | collective-permute-done | bytes 524320 | tf_op jit(solution)/shard_map/ppermute | solution.py:10
  76.1 6.1 collective-permute-start.10
  82.2 6.6 collective-permute-done.10
  89.1 25.0 %collective-permute-start.11 = (bf16[2,128,1024]{2,1,0:T(8,128)(2,1)S(1)}, bf16[2,128,1024]{2,1,0:T(8,128)(2,1)S(1)}, u32[]{:S(2)}, u32[]{:S(2)}) collective-permute-start(bf16[2,128,1024]{2,1,0:T(8,128)(2,1)S(1)} %fusion.77), channel_id=1, source_target_pairs={{0,8},{1,9},{2,10},{3,11},{4,12},{5,13},{6,14},{7,15},{8,16},{9,17... | collective-permute-start | bytes 1572872 | tf_op jit(solution)/shard_map/ppermute | solution.py:10
  114.1 6.6 collective-permute-done.11
  120.9 5.7 collective-permute-start.12
  126.7 7.7 %collective-permute-done.12 = bf16[2,128,1024]{2,1,0:T(8,128)(2,1)S(1)} collective-permute-done((bf16[2,128,1024]{2,1,0:T(8,128)(2,1)S(1)}, bf16[2,128,1024]{2,1,0:T(8,128)(2,1)S(1)}, u32[]{:S(2)}, u32[]{:S(2)}) %collective-permute-start.12) | collective-permute-done | bytes 524320 | tf_op jit(solution)/shard_map/ppermute | solution.py:10
  134.6 39.9 %collective-permute-start.13 = (bf16[2,128,1024]{2,1,0:T(8,128)(2,1)S(1)}, bf16[2,128,1024]{2,1,0:T(8,128)(2,1)S(1)}, u32[]{:S(2)}, u32[]{:S(2)}) collective-permute-start(bf16[2,128,1024]{2,1,0:T(8,128)(2,1)S(1)} %fusion.91), channel_id=1, source_target_pairs={{0,32},{1,33},{2,34},{3,35},{4,36},{5,37},{6,38},{7,39},{8,40},{9,... | collective-permute-start | bytes 1572872 | tf_op jit(solution)/shard_map/ppermute | solution.py:10
  175.1 10.6 %collective-permute-done.13 = bf16[2,128,1024]{2,1,0:T(8,128)(2,1)S(1)} collective-permute-done((bf16[2,128,1024]{2,1,0:T(8,128)(2,1)S(1)}, bf16[2,128,1024]{2,1,0:T(8,128)(2,1)S(1)}, u32[]{:S(2)}, u32[]{:S(2)}) %collective-permute-start.13) | collective-permute-done | bytes 524320 | tf_op jit(solution)/shard_map/ppermute | solution.py:10
  186.0 4.3 multiply_convert_fusion
  190.3 1.2 fusion.2
  192.4 2.1 add_convert_fusion.12
  194.5 1.5 collective-permute-start.14
  196.0 17.5 %collective-permute-done.14 = bf16[2,128,1024]{2,1,0:T(8,128)(2,1)S(1)} collective-permute-done((bf16[2,128,1024]{2,1,0:T(8,128)(2,1)S(1)}, bf16[2,128,1024]{2,1,0:T(8,128)(2,1)S(1)}, u32[]{:S(2)}, u32[]{:S(2)}) %collective-permute-start.14) | collective-permute-done | bytes 524320 | tf_op jit(solution)/shard_map/ppermute | solution.py:10
  213.8 1.3 collective-permute-start.15
  215.1 26.2 %collective-permute-done.15 = bf16[2,128,1024]{2,1,0:T(8,128)(2,1)S(1)} collective-permute-done((bf16[2,128,1024]{2,1,0:T(8,128)(2,1)S(1)}, bf16[2,128,1024]{2,1,0:T(8,128)(2,1)S(1)}, u32[]{:S(2)}, u32[]{:S(2)}) %collective-permute-start.15) | collective-permute-done | bytes 524320 | tf_op jit(solution)/shard_map/ppermute | solution.py:10
  242.0 1.3 collective-permute-start.16
  243.3 13.9 %collective-permute-done.16 = bf16[2,128,1024]{2,1,0:T(8,128)(2,1)S(1)} collective-permute-done((bf16[2,128,1024]{2,1,0:T(8,128)(2,1)S(1)}, bf16[2,128,1024]{2,1,0:T(8,128)(2,1)S(1)}, u32[]{:S(2)}, u32[]{:S(2)}) %collective-permute-start.16) | collective-permute-done | bytes 524320 | tf_op jit(solution)/shard_map/ppermute | solution.py:10
  258.3 1.3 collective-permute-start.17
  259.6 24.6 %collective-permute-done.17 = bf16[2,128,1024]{2,1,0:T(8,128)(2,1)S(1)} collective-permute-done((bf16[2,128,1024]{2,1,0:T(8,128)(2,1)S(1)}, bf16[2,128,1024]{2,1,0:T(8,128)(2,1)S(1)}, u32[]{:S(2)}, u32[]{:S(2)}) %collective-permute-start.17) | collective-permute-done | bytes 524320 | tf_op jit(solution)/shard_map/ppermute | solution.py:10
  284.5 1.3 collective-permute-start.18
  285.8 12.3 %collective-permute-done.18 = bf16[2,128,1024]{2,1,0:T(8,128)(2,1)S(1)} collective-permute-done((bf16[2,128,1024]{2,1,0:T(8,128)(2,1)S(1)}, bf16[2,128,1024]{2,1,0:T(8,128)(2,1)S(1)}, u32[]{:S(2)}, u32[]{:S(2)}) %collective-permute-start.18) | collective-permute-done | bytes 524320 | tf_op jit(solution)/shard_map/ppermute | solution.py:10
  298.1 2.0 fusion.73
  300.4 1.3 collective-permute-start.19
  301.7 2.5 collective-permute-done.19
  304.9 1.3 collective-permute-start.20
  306.2 8.8 %collective-permute-done.20 = bf16[2,64,1024]{2,1,0:T(8,128)(2,1)S(1)} collective-permute-done((bf16[2,64,1024]{2,1,0:T(8,128)(2,1)S(1)}, bf16[2,64,1024]{2,1,0:T(8,128)(2,1)S(1)}, u32[]{:S(2)}, u32[]{:S(2)}) %collective-permute-start.20) | collective-permute-done | bytes 262176 | tf_op jit(solution)/shard_map/ppermute | solution.py:10
  315.0 1.2 fusion.52
  316.5 1.3 collective-permute-start.21
  317.9 6.2 collective-permute-done.21
  324.8 1.3 collective-permute-start.22
  326.2 4.9 collective-permute-done.22
  331.0 1.3 fusion.38
  332.6 1.3 collective-permute-start.23
  333.9 4.2 collective-permute-done.23
  338.9 1.5 collective-permute-start.24
  340.4 2.7 multiply_reduce_fusion
  344.1 1.4 fusion.24
  345.5 1.0 copy-done.1
  346.8 1.3 collective-permute-start.25
  349.0 1.3 stack.65
  350.4 1.5 collective-permute-done.25
  351.8 2.0 fusion.17
  354.8 5.9 fusion.112
  361.0 1.3 collective-permute-start.26
  362.4 3.5 collective-permute-done.26
  366.0 1.2 fusion.123
  367.2 177.6 %all-reduce.3.cloned.1.call-done = (f32[2,1024]{1,0:T(2,128)}, f32[14,1024]{1,0:T(8,128)}) async-done(((f32[2,1024]{1,0:T(2,128)}, f32[14,1024]{1,0:T(8,128)}), (f32[2,1024]{1,0:T(2,128)}, f32[14,1024]{1,0:T(8,128)})) %all-reduce.3.cloned.1.call-update) | async-done | bytes 65552 | tf_op jit(solution)/shard_map/psum | solution.py:128
  546.3 1.3 multiply_bitcast_fusion.1
  547.6 150.3 %reduce-scatter.2.cloned.1.call-done = f32[16,2048]{1,0:T(8,128)} async-done(((f32[1024,2048]{1,0:T(8,128)}), f32[16,2048]{1,0:T(8,128)}) %reduce-scatter.2.cloned.1.call-update) | async-done | bytes 131088 | tf_op jit(solution)/shard_map/reduce_scatter | solution.py:85
  697.9 1.6 multiply_bitcast_fusion
  (95 shorter events, 20.0 us)
Async XLA Ops:
  7.2 537.6 %all-reduce.3.cloned.1.call-start = ((), (), s32[]{:S(2)}) async-start(), calls=%async_computation.2 | async-start | bytes 147456 | tf_op jit(solution)/shard_map/psum | solution.py:128
  8.0 2.8 collective-permute-start.1
  12.3 4.6 collective-permute-start.2
  17.1 4.7 collective-permute-start.3
  22.2 5.1 collective-permute-start.4
  27.4 5.3 collective-permute-start.5
  32.9 5.6 collective-permute-start.6
  38.8 6.4 collective-permute-start.7
  45.4 129.1 %copy-start.10 = (bf16[1,2,128,1024]{3,2,1,0:T(8,128)(2,1)S(1)}, bf16[1,2,128,1024]{3,2,1,0:T(8,128)(2,1)}, u32[]{:S(2)}) copy-start(bf16[1,2,128,1024]{3,2,1,0:T(8,128)(2,1)} %param.6) | copy-start | bytes 1572868
  45.4 129.7 %copy-start.7 = (f32[1,14,1024]{2,0,1:T(1,128)S(1)}, f32[1,14,1024]{2,0,1:T(1,128)}, u32[]{:S(2)}) copy-start(f32[1,14,1024]{2,0,1:T(1,128)} %param.8) | copy-start | bytes 172036
  45.5 8.2 %collective-permute-start.8 = (bf16[2,128,1024]{2,1,0:T(8,128)(2,1)S(1)}, bf16[2,128,1024]{2,1,0:T(8,128)(2,1)S(1)}, u32[]{:S(2)}, u32[]{:S(2)}) collective-permute-start(bf16[2,128,1024]{2,1,0:T(8,128)(2,1)S(1)} %fusion.56), channel_id=1, source_target_pairs={{0,1},{1,2},{2,3},{3,4},{4,5},{5,6},{6,7},{7,8},{8,9},{9,10},{10,1... | collective-permute-start | bytes 1572872 | tf_op jit(solution)/shard_map/ppermute | solution.py:10
  53.8 132.2 %copy-start = (bf16[1,2,128,1024]{3,2,1,0:T(8,128)(2,1)S(1)}, bf16[1,2,128,1024]{3,2,1,0:T(8,128)(2,1)}, u32[]{:S(2)}) copy-start(bf16[1,2,128,1024]{3,2,1,0:T(8,128)(2,1)} %param.5) | copy-start | bytes 1572868
  53.8 22.0 %collective-permute-start.9 = (bf16[2,128,1024]{2,1,0:T(8,128)(2,1)S(1)}, bf16[2,128,1024]{2,1,0:T(8,128)(2,1)S(1)}, u32[]{:S(2)}, u32[]{:S(2)}) collective-permute-start(bf16[2,128,1024]{2,1,0:T(8,128)(2,1)S(1)} %fusion.63), channel_id=1, source_target_pairs={{0,2},{1,3},{2,4},{3,5},{4,6},{5,7},{6,8},{7,9},{8,10},{9,11},{10,... | collective-permute-start | bytes 1572872 | tf_op jit(solution)/shard_map/ppermute | solution.py:10
  76.1 12.8 %collective-permute-start.10 = (bf16[2,128,1024]{2,1,0:T(8,128)(2,1)S(1)}, bf16[2,128,1024]{2,1,0:T(8,128)(2,1)S(1)}, u32[]{:S(2)}, u32[]{:S(2)}) collective-permute-start(bf16[2,128,1024]{2,1,0:T(8,128)(2,1)S(1)} %fusion.70), channel_id=1, source_target_pairs={{0,4},{1,5},{2,6},{3,7},{4,8},{5,9},{6,10},{7,11},{8,12},{9,13},{1... | collective-permute-start | bytes 1572872 | tf_op jit(solution)/shard_map/ppermute | solution.py:10
  89.1 31.6 %collective-permute-start.11 = (bf16[2,128,1024]{2,1,0:T(8,128)(2,1)S(1)}, bf16[2,128,1024]{2,1,0:T(8,128)(2,1)S(1)}, u32[]{:S(2)}, u32[]{:S(2)}) collective-permute-start(bf16[2,128,1024]{2,1,0:T(8,128)(2,1)S(1)} %fusion.77), channel_id=1, source_target_pairs={{0,8},{1,9},{2,10},{3,11},{4,12},{5,13},{6,14},{7,15},{8,16},{9,17... | collective-permute-start | bytes 1572872 | tf_op jit(solution)/shard_map/ppermute | solution.py:10
  120.9 13.4 %collective-permute-start.12 = (bf16[2,128,1024]{2,1,0:T(8,128)(2,1)S(1)}, bf16[2,128,1024]{2,1,0:T(8,128)(2,1)S(1)}, u32[]{:S(2)}, u32[]{:S(2)}) collective-permute-start(bf16[2,128,1024]{2,1,0:T(8,128)(2,1)S(1)} %fusion.84), channel_id=1, source_target_pairs={{0,16},{1,17},{2,18},{3,19},{4,20},{5,21},{6,22},{7,23},{8,24},{9,... | collective-permute-start | bytes 1572872 | tf_op jit(solution)/shard_map/ppermute | solution.py:10
  134.6 51.2 %collective-permute-start.13 = (bf16[2,128,1024]{2,1,0:T(8,128)(2,1)S(1)}, bf16[2,128,1024]{2,1,0:T(8,128)(2,1)S(1)}, u32[]{:S(2)}, u32[]{:S(2)}) collective-permute-start(bf16[2,128,1024]{2,1,0:T(8,128)(2,1)S(1)} %fusion.91), channel_id=1, source_target_pairs={{0,32},{1,33},{2,34},{3,35},{4,36},{5,37},{6,38},{7,39},{8,40},{9,... | collective-permute-start | bytes 1572872 | tf_op jit(solution)/shard_map/ppermute | solution.py:10
  174.5 17.0 %collective-permute-start = (bf16[1,2,128,1024]{3,2,1,0:T(8,128)(2,1)S(1)}, bf16[1,2,128,1024]{3,2,1,0:T(8,128)(2,1)S(1)}, u32[]{:S(2)}, u32[]{:S(2)}) collective-permute-start(bf16[1,2,128,1024]{3,2,1,0:T(8,128)(2,1)S(1)} %copy-done.10), channel_id=1, source_target_pairs={{0,192},{64,0},{128,64},{192,128},{1,193},{65,1},{129,65},{193,129... | collective-permute-start | bytes 1572872 | tf_op jit(solution)/shard_map/ppermute | solution.py:16
  186.0 4.3 copy-start.9
  190.3 1.9 copy-start.2
  191.6 0.8 copy-start.5
  192.2 2.2 copy-start.3
  192.2 2.2 copy-start.4
  194.5 18.9 %collective-permute-start.14 = (bf16[2,128,1024]{2,1,0:T(8,128)(2,1)S(1)}, bf16[2,128,1024]{2,1,0:T(8,128)(2,1)S(1)}, u32[]{:S(2)}, u32[]{:S(2)}) collective-permute-start(bf16[2,128,1024]{2,1,0:T(8,128)(2,1)S(1)} %get-tuple-element.169), channel_id=1, source_target_pairs={{32,0},{33,1},{34,2},{35,3},{36,4},{37,5},{38,6},{39,7},{40,8},{41... | collective-permute-start | bytes 1572872 | tf_op jit(solution)/shard_map/ppermute | solution.py:10
  213.8 27.5 %collective-permute-start.15 = (bf16[2,128,1024]{2,1,0:T(8,128)(2,1)S(1)}, bf16[2,128,1024]{2,1,0:T(8,128)(2,1)S(1)}, u32[]{:S(2)}, u32[]{:S(2)}) collective-permute-start(bf16[2,128,1024]{2,1,0:T(8,128)(2,1)S(1)} %add_convert_fusion.11), channel_id=1, source_target_pairs={{16,0},{17,1},{18,2},{19,3},{20,4},{21,5},{22,6},{23,7},{24,8},{25... | collective-permute-start | bytes 1572872 | tf_op jit(solution)/shard_map/ppermute | solution.py:10
  242.0 15.2 %collective-permute-start.16 = (bf16[2,128,1024]{2,1,0:T(8,128)(2,1)S(1)}, bf16[2,128,1024]{2,1,0:T(8,128)(2,1)S(1)}, u32[]{:S(2)}, u32[]{:S(2)}) collective-permute-start(bf16[2,128,1024]{2,1,0:T(8,128)(2,1)S(1)} %add_convert_fusion.10), channel_id=1, source_target_pairs={{8,0},{9,1},{10,2},{11,3},{12,4},{13,5},{14,6},{15,7},{16,8},{17,9... | collective-permute-start | bytes 1572872 | tf_op jit(solution)/shard_map/ppermute | solution.py:10
  258.3 25.9 %collective-permute-start.17 = (bf16[2,128,1024]{2,1,0:T(8,128)(2,1)S(1)}, bf16[2,128,1024]{2,1,0:T(8,128)(2,1)S(1)}, u32[]{:S(2)}, u32[]{:S(2)}) collective-permute-start(bf16[2,128,1024]{2,1,0:T(8,128)(2,1)S(1)} %add_convert_fusion.9), channel_id=1, source_target_pairs={{4,0},{5,1},{6,2},{7,3},{8,4},{9,5},{10,6},{11,7},{12,8},{13,9},{1... | collective-permute-start | bytes 1572872 | tf_op jit(solution)/shard_map/ppermute | solution.py:10
  284.5 13.6 %collective-permute-start.18 = (bf16[2,128,1024]{2,1,0:T(8,128)(2,1)S(1)}, bf16[2,128,1024]{2,1,0:T(8,128)(2,1)S(1)}, u32[]{:S(2)}, u32[]{:S(2)}) collective-permute-start(bf16[2,128,1024]{2,1,0:T(8,128)(2,1)S(1)} %get-tuple-element.139), channel_id=1, source_target_pairs={{2,0},{3,1},{4,2},{5,3},{6,4},{7,5},{8,6},{9,7},{10,8},{11,9},{12,... | collective-permute-start | bytes 1572872 | tf_op jit(solution)/shard_map/ppermute | solution.py:10
  300.4 3.8 collective-permute-start.19
  304.9 10.1 %collective-permute-start.20 = (bf16[2,64,1024]{2,1,0:T(8,128)(2,1)S(1)}, bf16[2,64,1024]{2,1,0:T(8,128)(2,1)S(1)}, u32[]{:S(2)}, u32[]{:S(2)}) collective-permute-start(bf16[2,64,1024]{2,1,0:T(8,128)(2,1)S(1)} %get-tuple-element.146), channel_id=1, source_target_pairs={{1,0},{2,1},{3,2},{4,3},{5,4},{6,5},{7,6},{8,7},{9,8},{10,9},{11,1... | collective-permute-start | bytes 786440 | tf_op jit(solution)/shard_map/ppermute | solution.py:10
  316.5 7.5 %collective-permute-start.21 = (bf16[2,32,1024]{2,1,0:T(8,128)(2,1)S(1)}, bf16[2,32,1024]{2,1,0:T(8,128)(2,1)S(1)}, u32[]{:S(2)}, u32[]{:S(2)}) collective-permute-start(bf16[2,32,1024]{2,1,0:T(8,128)(2,1)S(1)} %slice.233), channel_id=1, source_target_pairs={{1,0},{2,1},{3,2},{4,3},{5,4},{6,5},{7,6},{8,7},{9,8},{10,9},{11,1... | collective-permute-start | bytes 393224 | tf_op jit(solution)/shard_map/ppermute | solution.py:10
  324.8 6.2 collective-permute-start.22
  332.6 5.5 collective-permute-start.23
  338.9 5.2 collective-permute-start.24
  345.5 1.0 copy-start.1
  346.5 7.4 %copy-start.8 = (f32[1,2,1024]{2,1,0:T(2,128)S(1)}, f32[1,2,1024]{2,1,0:T(2,128)}, u32[]{:S(2)}) copy-start(f32[1,2,1024]{2,1,0:T(2,128)} %param.7) | copy-start | bytes 24580
  346.8 5.0 collective-permute-start.25
  354.8 343.1 %reduce-scatter.2.cloned.1.call-start = ((), (), s32[]{:S(2)}) async-start(), calls=%async_computation.1 | async-start | bytes 8519680 | tf_op jit(solution)/shard_map/reduce_scatter | solution.py:85
  360.7 5.3 copy-start.6
  361.0 5.0 collective-permute-start.26
Sparse Core Ops, SparseCore 0:
  354.9 189.7 all-reduce.2
  549.0 148.8 reduce-scatter.1
where the time goes:
time: 707 us; the launch traced here: 706 us
  waiting for transfers between devices  504 us (71%)
  starting transfers between devices  141 us (20%)
  other arithmetic  31.5 us (4%)
  between operations  14.8 us (2%)
  matrix products  9.17 us (1%)
    psum x1, waiting for transfers between devices, shards(): lax.psum((angle_terms, jnp.stack(level_grads)), 'seq')  178 us
    ppermute x26, waiting for transfers between devices, shifted_2(): return lax.ppermute(block, axis, route)  176 us
    reduce_scatter x1, waiting for transfers between devices, shards(): lax.psum_scatter(jnp.einsum('rc,rk->ck', activated, grad_proj, preferred_...  150 us
    ppermute x26, starting transfers between devices, shifted_2(): return lax.ppermute(block, axis, route)  140 us
  transfers between devices with their start and end apart: 29, of which 27 were waited for; matrix products, arithmetic and copies ran while one was open for 3% of the time, Pallas kernels for 0%

commit v1 on v0

--- a/solution.py
+++ b/solution.py
@@ -20,9 +20,20 @@
     return lax.optimization_barrier(values.astype(jnp.bfloat16))
 
 
-def near_behind(state_now, spacing, positions):
-    rim_rows = shifted_2(state_now[:, positions - spacing :, :], "seq", 1)
-    return jnp.concatenate([rim_rows, state_now[:, : positions - spacing, :]], axis=1)
+def behind(values, spacing):
+    return jnp.pad(values, ((0, 0), (spacing, 0), (0, 0)))[:, : values.shape[1], :]
+
+
+def butterfly_sum(value, axis):
+    count = lax.axis_size(axis)
+    if count & (count - 1):
+        return lax.psum(value, axis)
+    step = 1
+    while step < count:
+        pairs = [(i, i ^ step) for i in range(count)]
+        value = value + lax.ppermute(value, axis, pairs)
+        step *= 2
+    return value
 
 
 def tap_terms(totals, adjoint, weighted, current, previous):
@@ -51,16 +62,20 @@
     states = []
     shifted_states = []
     mixed = jnp.zeros(activations.shape, jnp.float32)
-    state_now = activations
+    halo = shifted_2(activations, "seq", 1)
+    wide_state = jnp.concatenate([halo, activations], axis=1)
     for level_idx in range(near_count):
         spacing = 2**level_idx
-        shifted = near_behind(state_now, spacing, positions)
-        current = state_now.astype(jnp.float32)
-        previous = shifted.astype(jnp.float32)
+        wide_shifted = behind(wide_state, spacing)
+        wide_current = wide_state.astype(jnp.float32)
+        wide_previous = wide_shifted.astype(jnp.float32)
+        current = wide_current[:, positions:, :]
+        previous = wide_previous[:, positions:, :]
         mixed = mixed + weights[level_idx] * (c_high * current + s_high * previous)
-        states.append(state_now)
-        shifted_states.append(shifted)
-        state_now = rounded(c_low * current + s_low * previous)
+        states.append(wide_state[:, positions:, :])
+        shifted_states.append(wide_shifted[:, positions:, :])
+        wide_state = rounded(c_low * wide_current + s_low * wide_previous)
+    state_now = wide_state[:, positions:, :]
     for level_idx in range(near_count, levels):
         spacing = 2**level_idx
         shifted = shifted_2(state_now, "seq", spacing // positions)
@@ -109,6 +124,23 @@
         carried = rounded(s_low * adjoint + s_high * weighted)
         arrived = shifted_2(carried, "seq", -(spacing // positions)).astype(jnp.float32)
         adjoint = c_low * adjoint + c_high * weighted + arrived
+    fronts = []
+    front_adjoint = adjoint
+    for level_idx in reversed(range(near_count)):
+        spacing = 2**level_idx
+        span = 2 * spacing
+        part = grad_conv[:, :span, :]
+        weighted = weights[level_idx] * part
+        carried = rounded(s_low * front_adjoint[:, :span, :] + s_high * weighted)
+        fronts.append(carried[:, :spacing, :])
+        if level_idx > 0:
+            front_adjoint = (
+                c_low * front_adjoint[:, :spacing, :]
+                + c_high * weighted[:, :spacing, :]
+                + carried[:, spacing:, :].astype(jnp.float32)
+            )
+    rims = shifted_2(jnp.concatenate(fronts, axis=1), "seq", -1)
+    offset = 0
     for level_idx in reversed(range(near_count)):
         spacing = 2**level_idx
         current = states[level_idx].astype(jnp.float32)
@@ -119,13 +151,16 @@
         )
         totals = tap_terms(totals, adjoint, weighted, current, previous)
         carried = rounded(s_low * adjoint + s_high * weighted)
-        rim_rows = shifted_2(carried[:, :spacing, :], "seq", -1)
+        rim_rows = rims[:, offset : offset + spacing, :]
+        offset += spacing
         arrived = jnp.concatenate([carried[:, spacing:, :], rim_rows], axis=1).astype(jnp.float32)
         adjoint = c_low * adjoint + c_high * weighted + arrived
     angle_terms = jnp.stack(
         [c_low * totals[1] - s_low * totals[0], c_high * totals[3] - s_high * totals[2]]
     )
-    angle_total, level_total = lax.psum((angle_terms, jnp.stack(level_grads)), "seq")
+    summed = butterfly_sum(jnp.concatenate([angle_terms, jnp.stack(level_grads)], axis=0), "seq")
+    angle_total = summed[:2]
+    level_total = summed[2:]
     grad_input = (received.astype(jnp.float32) + adjoint).astype(jnp.bfloat16)
     return (
         grad_input[None],

time: 707 us -> 383 us (0.54)
  waiting for transfers between devices: 504 us -> 210 us
  starting transfers between devices: 141 us -> 80.2 us
  other arithmetic: 31.5 us -> 47.5 us
  local copies, waits for them, and re-layouts: 6.5 us -> 18 us
    psum x1 -> x0, waiting for transfers between devices: 178 us -> none  [shards(): lax.psum((angle_terms, jnp.stack(level_grads)), 'seq')]
    reduce_scatter x1, waiting for transfers between devices: 150 us -> 17.5 us  [shards(): lax.psum_scatter(jnp.einsum('rc,rk->ck', activated, grad_proj, preferred_...]
    ppermute x26 -> x14, starting transfers between devices: 140 us -> 55.6 us  [shifted_2(): return lax.ppermute(block, axis, route)]
    ppermute x0 -> x6, starting transfers between devices: none -> 24 us  [butterfly_sum(): value = value + lax.ppermute(value, axis, pairs)]
    ppermute x0 -> x6, waiting for transfers between devices: none -> 21 us  [butterfly_sum(): value = value + lax.ppermute(value, axis, pairs)]
    convert_element_type x0 -> x5, other arithmetic: none -> 8.3 us  [shards(): wide_current = wide_state.astype(jnp.float32)]
    ppermute x26 -> x14, waiting for transfers between devices: 176 us -> 172 us  [shifted_2(): return lax.ppermute(block, axis, route)]
  transfers between devices with their start and end apart: 29 -> 22, of which waited for: 27 -> 21; matrix products, arithmetic and copies ran while one was open for 3% -> 15% of each run, Pallas kernels for 0% -> 0%
where the time goes in v1:
time: 383 us; the launch traced here: 382 us
  waiting for transfers between devices  210 us (55%)
  starting transfers between devices  80.2 us (21%)
  other arithmetic  47.5 us (12%)
  local copies, waits for them, and re-layouts  18 us (5%)
  between operations  15.7 us (4%)
  matrix products  10.2 us (3%)
    ppermute x14, waiting for transfers between devices, shifted_2(): return lax.ppermute(block, axis, route)  172 us
    ppermute x14, starting transfers between devices, shifted_2(): return lax.ppermute(block, axis, route)  55.6 us
    ppermute x6, starting transfers between devices, butterfly_sum(): value = value + lax.ppermute(value, axis, pairs)  24 us
    ppermute x6, waiting for transfers between devices, butterfly_sum(): value = value + lax.ppermute(value, axis, pairs)  21 us
    reduce_scatter x1, waiting for transfers between devices, shards(): lax.psum_scatter(jnp.einsum('rc,rk->ck', activated, grad_proj, preferred_...  17.5 us
    reduce_sum x9, other arithmetic, tap_terms(): jnp.sum(adjoint * previous, axis=(0, 1))  10.7 us
    convert_element_type x30, other arithmetic, rounded(): return lax.optimization_barrier(values.astype(jnp.bfloat16))  8.96 us
    convert_element_type x5, other arithmetic, shards(): wide_current = wide_state.astype(jnp.float32)  8.3 us
  transfers between devices with their start and end apart: 22, of which 21 were waited for; matrix products, arithmetic and copies ran while one was open for 15% of the time, Pallas kernels for 0%

profile of v1, /device:TPU:2, one launch (start us, length us, event | category | flops | bytes accessed | tf_op | source)
XLA Modules:
  0.0 381.8 jit_solution(1377588354217517067)
XLA Ops:
  7.2 1.8 collective-permute-start.1
  9.0 1.0 slice_cosine_fusion
  10.0 0.7 collective-permute-done.1
  10.7 1.5 fusion.179
  15.1 8.6 %collective-permute-start.2 = (bf16[2,128,1024]{2,1,0:T(8,128)(2,1)S(1)}, bf16[2,128,1024]{2,1,0:T(8,128)(2,1)S(1)}, u32[]{:S(2)}, u32[]{:S(2)}) collective-permute-start(bf16[2,128,1024]{2,1,0:T(8,128)(2,1)S(1)} %slice.462), channel_id=1, source_target_pairs={{0,1},{1,2},{2,3},{3,4},{4,5},{5,6},{6,7},{7,8},{8,9},{9,10},{10,1... | collective-permute-start | bytes 1572872 | tf_op jit(solution)/shard_map/ppermute | solution.py:10
  23.7 1.5 collective-permute-done.2
  25.5 11.3 %collective-permute-start.3 = (bf16[2,128,1024]{2,1,0:T(8,128)(2,1)S(1)}, bf16[2,128,1024]{2,1,0:T(8,128)(2,1)S(1)}, u32[]{:S(2)}, u32[]{:S(2)}) collective-permute-start(bf16[2,128,1024]{2,1,0:T(8,128)(2,1)S(1)} %fusion.70), channel_id=1, source_target_pairs={{0,2},{1,3},{2,4},{3,5},{4,6},{5,7},{6,8},{7,9},{8,10},{9,11},{10,... | collective-permute-start | bytes 1572872 | tf_op jit(solution)/shard_map/ppermute | solution.py:10
  36.7 10.5 %collective-permute-done.3 = bf16[2,128,1024]{2,1,0:T(8,128)(2,1)S(1)} collective-permute-done((bf16[2,128,1024]{2,1,0:T(8,128)(2,1)S(1)}, bf16[2,128,1024]{2,1,0:T(8,128)(2,1)S(1)}, u32[]{:S(2)}, u32[]{:S(2)}) %collective-permute-start.3) | collective-permute-done | bytes 524320 | tf_op jit(solution)/shard_map/ppermute | solution.py:10
  47.5 6.2 %collective-permute-start.4 = (bf16[2,128,1024]{2,1,0:T(8,128)(2,1)S(1)}, bf16[2,128,1024]{2,1,0:T(8,128)(2,1)S(1)}, u32[]{:S(2)}, u32[]{:S(2)}) collective-permute-start(bf16[2,128,1024]{2,1,0:T(8,128)(2,1)S(1)} %fusion.77), channel_id=1, source_target_pairs={{0,4},{1,5},{2,6},{3,7},{4,8},{5,9},{6,10},{7,11},{8,12},{9,13},{1... | collective-permute-start | bytes 1572872 | tf_op jit(solution)/shard_map/ppermute | solution.py:10
  53.7 11.8 %collective-permute-done.4 = bf16[2,128,1024]{2,1,0:T(8,128)(2,1)S(1)} collective-permute-done((bf16[2,128,1024]{2,1,0:T(8,128)(2,1)S(1)}, bf16[2,128,1024]{2,1,0:T(8,128)(2,1)S(1)}, u32[]{:S(2)}, u32[]{:S(2)}) %collective-permute-start.4) | collective-permute-done | bytes 524320 | tf_op jit(solution)/shard_map/ppermute | solution.py:10
  65.7 4.1 %collective-permute-start.5 = (bf16[2,128,1024]{2,1,0:T(8,128)(2,1)S(1)}, bf16[2,128,1024]{2,1,0:T(8,128)(2,1)S(1)}, u32[]{:S(2)}, u32[]{:S(2)}) collective-permute-start(bf16[2,128,1024]{2,1,0:T(8,128)(2,1)S(1)} %fusion.84), channel_id=1, source_target_pairs={{0,8},{1,9},{2,10},{3,11},{4,12},{5,13},{6,14},{7,15},{8,16},{9,17... | collective-permute-start | bytes 1572872 | tf_op jit(solution)/shard_map/ppermute | solution.py:10
  70.6 9.9 %collective-permute-done.5 = bf16[2,128,1024]{2,1,0:T(8,128)(2,1)S(1)} collective-permute-done((bf16[2,128,1024]{2,1,0:T(8,128)(2,1)S(1)}, bf16[2,128,1024]{2,1,0:T(8,128)(2,1)S(1)}, u32[]{:S(2)}, u32[]{:S(2)}) %collective-permute-start.5) | collective-permute-done | bytes 524320 | tf_op jit(solution)/shard_map/ppermute | solution.py:10
  80.7 5.8 %collective-permute-start.6 = (bf16[2,128,1024]{2,1,0:T(8,128)(2,1)S(1)}, bf16[2,128,1024]{2,1,0:T(8,128)(2,1)S(1)}, u32[]{:S(2)}, u32[]{:S(2)}) collective-permute-start(bf16[2,128,1024]{2,1,0:T(8,128)(2,1)S(1)} %fusion.91), channel_id=1, source_target_pairs={{0,16},{1,17},{2,18},{3,19},{4,20},{5,21},{6,22},{7,23},{8,24},{9,... | collective-permute-start | bytes 1572872 | tf_op jit(solution)/shard_map/ppermute | solution.py:10
  86.5 2.9 fusion.186
  89.4 1.1 fusion.189
  90.5 6.2 %collective-permute-done.6 = bf16[2,128,1024]{2,1,0:T(8,128)(2,1)S(1)} collective-permute-done((bf16[2,128,1024]{2,1,0:T(8,128)(2,1)S(1)}, bf16[2,128,1024]{2,1,0:T(8,128)(2,1)S(1)}, u32[]{:S(2)}, u32[]{:S(2)}) %collective-permute-start.6) | collective-permute-done | bytes 524320 | tf_op jit(solution)/shard_map/ppermute | solution.py:10
  96.9 7.9 %collective-permute-start.7 = (bf16[2,128,1024]{2,1,0:T(8,128)(2,1)S(1)}, bf16[2,128,1024]{2,1,0:T(8,128)(2,1)S(1)}, u32[]{:S(2)}, u32[]{:S(2)}) collective-permute-start(bf16[2,128,1024]{2,1,0:T(8,128)(2,1)S(1)} %fusion.98), channel_id=1, source_target_pairs={{0,32},{1,33},{2,34},{3,35},{4,36},{5,37},{6,38},{7,39},{8,40},{9,... | collective-permute-start | bytes 1572872 | tf_op jit(solution)/shard_map/ppermute | solution.py:10
  104.7 1.7 fusion.191
  106.5 1.1 fusion.187
  107.6 3.7 collective-permute-done.7
  111.6 5.3 %multiply_convert_fusion = (bf16[2,128,1024]{2,1,0:T(8,128)(2,1)S(1)}, f32[2,128,1024]{2,1,0:T(8,128)S(1)}) fusion(bf16[2,128,1024]{2,1,0:T(8,128)(2,1)S(1)} %fusion.105, f32[1024]{0:T(1024)S(1)} %bitcast.219, bf16[2,128,1024]{2,1,0:T(8,128)(2,1)S(1)} %collective-permute-done.7, bf16[2,128,1024]{2,1,0:T(8,128)(2,1)S(1)} %fusion.98, f32[1024]{0:T(1024)S(1)} %bitcast.225, ...), kind=kLoop, calls=%fused_computation.312 | loop fusion | flops 23068672 | bytes 23134208 | tf_op jit(solution)/shard_map/convert_element_type | solution.py:90
  116.9 3.6 fusion.2
  120.5 1.6 fusion.151
  122.1 2.0 add_convert_fusion.19
  124.1 1.3 collective-permute-start.8
  125.4 21.5 %collective-permute-done.8 = bf16[2,128,1024]{2,1,0:T(8,128)(2,1)S(1)} collective-permute-done((bf16[2,128,1024]{2,1,0:T(8,128)(2,1)S(1)}, bf16[2,128,1024]{2,1,0:T(8,128)(2,1)S(1)}, u32[]{:S(2)}, u32[]{:S(2)}) %collective-permute-start.8) | collective-permute-done | bytes 524320 | tf_op jit(solution)/shard_map/ppermute | solution.py:10
  147.4 1.3 collective-permute-start.9
  148.7 30.4 %collective-permute-done.9 = bf16[2,128,1024]{2,1,0:T(8,128)(2,1)S(1)} collective-permute-done((bf16[2,128,1024]{2,1,0:T(8,128)(2,1)S(1)}, bf16[2,128,1024]{2,1,0:T(8,128)(2,1)S(1)}, u32[]{:S(2)}, u32[]{:S(2)}) %collective-permute-start.9) | collective-permute-done | bytes 524320 | tf_op jit(solution)/shard_map/ppermute | solution.py:10
  179.1 0.8 copy-done.36
  179.9 1.4 add_convert_fusion.17
  181.4 1.3 collective-permute-start.10
  182.6 4.5 %fusion.145 = f32[1024,2048]{1,0:T(8,128)} fusion(bf16[256,1024]{1,0:T(8,128)(2,1)S(1)} %bitcast.206, bf16[256,1024]{1,0:T(8,128)(2,1)S(1)} %get-tuple-element.147, bf16[256,1024]{1,0:T(8,128)(2,1)S(1)} %get-tuple-element.146), kind=kOutput, calls=%fused_computation.272 | convolution fusion | flops 1075838976 | bytes 9961472 | tf_op jit(solution)/shard_map/rc,rk->ck/dot_general | solution.py:101
  187.2 36.7 %collective-permute-done.10 = bf16[2,128,1024]{2,1,0:T(8,128)(2,1)} collective-permute-done((bf16[2,128,1024]{2,1,0:T(8,128)(2,1)}, bf16[2,128,1024]{2,1,0:T(8,128)(2,1)}, u32[]{:S(2)}, u32[]{:S(2)}) %collective-permute-start.10) | collective-permute-done | bytes 524320 | tf_op jit(solution)/shard_map/ppermute | solution.py:10
  223.9 4.3 %fusion.87 = (f32[1024]{0:T(1024)}, f32[1024]{0:T(1024)}, f32[1024]{0:T(1024)}, f32[1024]{0:T(1024)}, f32[1024]{0:T(1024)}, /*index=5*/f32[1024]{0:T(1024)}, f32...) fusion(bf16[2,128,1024]{2,1,0:T(8,128)(2,1)} %copy-done.28, ...), kind=kLoop, calls=%fused_computation.198 | loop fusion | flops 15455232 | bytes 6901760 | tf_op jit(solution)/shard_map/reduce_sum | solution.py:42
  228.4 1.4 collective-permute-start.11
  229.9 15.5 %collective-permute-done.11 = bf16[2,128,1024]{2,1,0:T(8,128)(2,1)S(1)} collective-permute-done((bf16[2,128,1024]{2,1,0:T(8,128)(2,1)S(1)}, bf16[2,128,1024]{2,1,0:T(8,128)(2,1)S(1)}, u32[]{:S(2)}, u32[]{:S(2)}) %collective-permute-start.11) | collective-permute-done | bytes 524320 | tf_op jit(solution)/shard_map/ppermute | solution.py:10
  245.4 2.4 fusion.80
  248.1 1.8 collective-permute-start.12
  249.9 16.8 %collective-permute-done.12 = bf16[2,128,1024]{2,1,0:T(8,128)(2,1)S(1)} collective-permute-done((bf16[2,128,1024]{2,1,0:T(8,128)(2,1)S(1)}, bf16[2,128,1024]{2,1,0:T(8,128)(2,1)S(1)}, u32[]{:S(2)}, u32[]{:S(2)}) %collective-permute-start.12) | collective-permute-done | bytes 524320 | tf_op jit(solution)/shard_map/ppermute | solution.py:10
  266.7 1.1 fusion.73
  267.8 2.3 multiply_reduce_fusion.5
  270.1 1.3 collective-permute-start.13
  271.4 2.6 collective-permute-done.13
  274.0 1.2 fusion.20
  280.0 0.7 fusion.192
  280.7 6.5 %concatenate.46 = bf16[2,127,1024]{2,1,0:T(8,128)(2,1)} concatenate(bf16[2,64,1024]{2,1,0:T(8,128)(2,1)} %get-tuple-element.164, bf16[2,32,1024]{2,1,0:T(8,128)(2,1)S(1)} %slice.470, bf16[2,16,1024]{2,1,0:T(8,128)(2,1)} %slice.475, bf16[2,8,1024]{2,1,0:T(8,128)(2,1)} %slice.480, bf16[2,4,1024]{2,1,0:T(4,128)(2,1)} %slice.485, bf16[2,2,1024]{2,1,0:T(2,128)(2,1)} %slice.490, ...), dimensions={1} | concatenate | bytes 1040384 | tf_op jit(solution)/shard_map/concatenate | solution.py:142
  287.5 1.6 collective-permute-start.14
  289.0 4.4 %multiply_reduce_fusion = (f32[1024]{0:T(1024)S(1)}, f32[1024]{0:T(1024)S(1)}, f32[1024]{0:T(1024)S(1)}, f32[1024]{0:T(1024)S(1)}, f32[1024]{0:T(1024)S(1)}, /*i...) fusion(f32[2,128,1024]{2,1,0:T(8,128)S(1)} %get-tuple-element.1, ...), kind=kLoop, calls=%fused_computation.281 | loop fusion | flops 18070528 | bytes 6914048 | tf_op jit(solution)/shard_map/reduce_sum | solution.py:120
  293.6 4.1 %collective-permute-done.14 = bf16[2,127,1024]{2,1,0:T(8,128)(2,1)S(1)} collective-permute-done((bf16[2,127,1024]{2,1,0:T(8,128)(2,1)}, bf16[2,127,1024]{2,1,0:T(8,128)(2,1)S(1)}, u32[]{:S(2)}, u32[]{:S(2)}) %collective-permute-start.14) | collective-permute-done | bytes 520224 | tf_op jit(solution)/shard_map/ppermute | solution.py:10
  298.8 0.7 copy-done.2
  302.5 0.7 copy-done.10
  306.2 18.9 %collective-permute-start.15 = (f32[16,1024]{1,0:T(8,128)S(1)}, f32[16,1024]{1,0:T(8,128)S(1)}, u32[]{:S(2)}, u32[]{:S(2)}) collective-permute-start(f32[16,1024]{1,0:T(8,128)S(1)} %concatenate.54), channel_id=1, source_target_pairs={{0,1},{1,0},{2,3},{3,2},{4,5},{5,4},{6,7},{7,6},{8,9},{9,8},{10,11... | collective-permute-start | bytes 196616 | tf_op jit(solution)/shard_map/ppermute | solution.py:34
  325.1 0.9 collective-permute-done.15
  326.1 4.3 %collective-permute-done.16 = f32[16,1024]{1,0:T(8,128)S(1)} collective-permute-done((f32[16,1024]{1,0:T(8,128)S(1)}, f32[16,1024]{1,0:T(8,128)S(1)}, u32[]{:S(2)}, u32[]{:S(2)}) %collective-permute-start.16) | collective-permute-done | bytes 65568 | tf_op jit(solution)/shard_map/ppermute | solution.py:34
  330.4 3.5 collective-permute-start.17
  333.9 2.7 collective-permute-done.17
  336.6 1.0 collective-permute-start.18
  337.6 3.3 collective-permute-done.18
  341.8 0.8 slice.508
  342.5 3.7 collective-permute-done.19
  346.3 2.2 fusion.156
  348.5 6.1 %collective-permute-done.20 = f32[16,1024]{1,0:T(8,128)S(1)} collective-permute-done((f32[16,1024]{1,0:T(8,128)S(1)}, f32[16,1024]{1,0:T(8,128)S(1)}, u32[]{:S(2)}, u32[]{:S(2)}) %collective-permute-start.20) | collective-permute-done | bytes 65568 | tf_op jit(solution)/shard_map/ppermute | solution.py:34
  355.9 17.5 %reduce-scatter.2.cloned.1.call-done = f32[16,2048]{1,0:T(8,128)} async-done(((f32[1024,2048]{1,0:T(8,128)}), f32[16,2048]{1,0:T(8,128)}) %reduce-scatter.2.cloned.1.call-update) | async-done | bytes 131088 | tf_op jit(solution)/shard_map/reduce_scatter | solution.py:100
  373.4 1.6 multiply_bitcast_fusion
  (275 shorter events, 19.5 us)
Async XLA Ops:
  7.2 366.2 %reduce-scatter.2.cloned.1.call-start = ((), (), s32[]{:S(2)}) async-start(), calls=%async_computation.1 | async-start | bytes 8519680 | tf_op jit(solution)/shard_map/reduce_scatter | solution.py:100
  7.2 3.5 collective-permute-start.1
  12.7 73.8 %copy-start.8 = (bf16[2,256,1024]{2,1,0:T(8,128)(2,1)}, bf16[2,256,1024]{2,1,0:T(8,128)(2,1)S(1)}, u32[]{:S(2)}) copy-start(bf16[2,256,1024]{2,1,0:T(8,128)(2,1)S(1)} %add_convert_fusion.6) | copy-start | bytes 3145732
  13.9 75.4 %copy-start = (bf16[2,256,1024]{2,1,0:T(8,128)(2,1)}, bf16[2,256,1024]{2,1,0:T(8,128)(2,1)S(1)}, u32[]{:S(2)}) copy-start(bf16[2,256,1024]{2,1,0:T(8,128)(2,1)S(1)} %add_convert_fusion.3) | copy-start | bytes 3145732
  14.3 75.1 %copy-start.3 = (bf16[2,256,1024]{2,1,0:T(8,128)(2,1)}, bf16[2,256,1024]{2,1,0:T(8,128)(2,1)S(1)}, u32[]{:S(2)}) copy-start(bf16[2,256,1024]{2,1,0:T(8,128)(2,1)S(1)} %add_convert_fusion.2) | copy-start | bytes 3145732
  14.7 90.1 %copy-start.6 = (bf16[2,256,1024]{2,1,0:T(8,128)(2,1)}, bf16[2,256,1024]{2,1,0:T(8,128)(2,1)S(1)}, u32[]{:S(2)}) copy-start(bf16[2,256,1024]{2,1,0:T(8,128)(2,1)S(1)} %add_convert_fusion.1) | copy-start | bytes 3145732
  15.0 96.4 %copy-start.13 = (bf16[2,256,1024]{2,1,0:T(8,128)(2,1)}, bf16[2,256,1024]{2,1,0:T(8,128)(2,1)S(1)}, u32[]{:S(2)}) copy-start(bf16[2,256,1024]{2,1,0:T(8,128)(2,1)S(1)} %add_convert_fusion) | copy-start | bytes 3145732
  15.1 55.4 %copy-start.61 = (f32[1,14,1024]{2,0,1:T(1,128)S(1)}, f32[1,14,1024]{2,0,1:T(1,128)}, u32[]{:S(2)}) copy-start(f32[1,14,1024]{2,0,1:T(1,128)} %param.8) | copy-start | bytes 172036
  15.1 10.1 %collective-permute-start.2 = (bf16[2,128,1024]{2,1,0:T(8,128)(2,1)S(1)}, bf16[2,128,1024]{2,1,0:T(8,128)(2,1)S(1)}, u32[]{:S(2)}, u32[]{:S(2)}) collective-permute-start(bf16[2,128,1024]{2,1,0:T(8,128)(2,1)S(1)} %slice.462), channel_id=1, source_target_pairs={{0,1},{1,2},{2,3},{3,4},{4,5},{5,6},{6,7},{7,8},{8,9},{9,10},{10,1... | collective-permute-start | bytes 1572872 | tf_op jit(solution)/shard_map/ppermute | solution.py:10
  25.2 86.3 %copy-start.25 = (bf16[2,128,1024]{2,1,0:T(8,128)(2,1)}, bf16[2,128,1024]{2,1,0:T(8,128)(2,1)S(1)}, u32[]{:S(2)}) copy-start(bf16[2,128,1024]{2,1,0:T(8,128)(2,1)S(1)} %collective-permute-done.2) | copy-start | bytes 1572868
  25.4 86.1 %copy-start.23 = (bf16[2,128,1024]{2,1,0:T(8,128)(2,1)}, bf16[2,128,1024]{2,1,0:T(8,128)(2,1)S(1)}, u32[]{:S(2)}) copy-start(bf16[2,128,1024]{2,1,0:T(8,128)(2,1)S(1)} %fusion.70) | copy-start | bytes 1572868
  25.5 21.8 %collective-permute-start.3 = (bf16[2,128,1024]{2,1,0:T(8,128)(2,1)S(1)}, bf16[2,128,1024]{2,1,0:T(8,128)(2,1)S(1)}, u32[]{:S(2)}, u32[]{:S(2)}) collective-permute-start(bf16[2,128,1024]{2,1,0:T(8,128)(2,1)S(1)} %fusion.70), channel_id=1, source_target_pairs={{0,2},{1,3},{2,4},{3,5},{4,6},{5,7},{6,8},{7,9},{8,10},{9,11},{10,... | collective-permute-start | bytes 1572872 | tf_op jit(solution)/shard_map/ppermute | solution.py:10
  47.2 6.5 %copy-start.33 = (bf16[2,128,1024]{2,1,0:T(8,128)(2,1)}, bf16[2,128,1024]{2,1,0:T(8,128)(2,1)S(1)}, u32[]{:S(2)}) copy-start(bf16[2,128,1024]{2,1,0:T(8,128)(2,1)S(1)} %collective-permute-done.3) | copy-start | bytes 1572868
  47.5 64.1 %copy-start.19 = (bf16[2,128,1024]{2,1,0:T(8,128)(2,1)}, bf16[2,128,1024]{2,1,0:T(8,128)(2,1)S(1)}, u32[]{:S(2)}) copy-start(bf16[2,128,1024]{2,1,0:T(8,128)(2,1)S(1)} %fusion.77) | copy-start | bytes 1572868
  47.5 18.0 %collective-permute-start.4 = (bf16[2,128,1024]{2,1,0:T(8,128)(2,1)S(1)}, bf16[2,128,1024]{2,1,0:T(8,128)(2,1)S(1)}, u32[]{:S(2)}, u32[]{:S(2)}) collective-permute-start(bf16[2,128,1024]{2,1,0:T(8,128)(2,1)S(1)} %fusion.77), channel_id=1, source_target_pairs={{0,4},{1,5},{2,6},{3,7},{4,8},{5,9},{6,10},{7,11},{8,12},{9,13},{1... | collective-permute-start | bytes 1572872 | tf_op jit(solution)/shard_map/ppermute | solution.py:10
  65.5 46.0 %copy-start.28 = (bf16[2,128,1024]{2,1,0:T(8,128)(2,1)}, bf16[2,128,1024]{2,1,0:T(8,128)(2,1)S(1)}, u32[]{:S(2)}) copy-start(bf16[2,128,1024]{2,1,0:T(8,128)(2,1)S(1)} %collective-permute-done.4) | copy-start | bytes 1572868
  65.7 45.8 %copy-start.20 = (bf16[2,128,1024]{2,1,0:T(8,128)(2,1)}, bf16[2,128,1024]{2,1,0:T(8,128)(2,1)S(1)}, u32[]{:S(2)}) copy-start(bf16[2,128,1024]{2,1,0:T(8,128)(2,1)S(1)} %fusion.84) | copy-start | bytes 1572868
  65.7 14.8 %collective-permute-start.5 = (bf16[2,128,1024]{2,1,0:T(8,128)(2,1)S(1)}, bf16[2,128,1024]{2,1,0:T(8,128)(2,1)S(1)}, u32[]{:S(2)}, u32[]{:S(2)}) collective-permute-start(bf16[2,128,1024]{2,1,0:T(8,128)(2,1)S(1)} %fusion.84), channel_id=1, source_target_pairs={{0,8},{1,9},{2,10},{3,11},{4,12},{5,13},{6,14},{7,15},{8,16},{9,17... | collective-permute-start | bytes 1572872 | tf_op jit(solution)/shard_map/ppermute | solution.py:10
  69.9 50.6 %collective-permute-start = (bf16[1,2,128,1024]{3,2,1,0:T(8,128)(2,1)}, bf16[1,2,128,1024]{3,2,1,0:T(8,128)(2,1)}, u32[]{:S(2)}, u32[]{:S(2)}) collective-permute-start(bf16[1,2,128,1024]{3,2,1,0:T(8,128)(2,1)} %param.6), channel_id=1, source_target_pairs={{0,192},{64,0},{128,64},{192,128},{1,193},{65,1},{129,65},{193,129... | collective-permute-start | bytes 1572872 | tf_op jit(solution)/shard_map/ppermute | solution.py:16
  70.5 153.4 %copy-start.41 = (f32[1,1,1024]{2,0,1:T(1,128)}, f32[1,1,1024]{2,0,1:T(1,128)S(1)}, u32[]{:S(2)}) copy-start(f32[1,1,1024]{2,0,1:T(1,128)S(1)} %get-tuple-element.174) | copy-start | bytes 12292
  70.5 153.4 %copy-start.44 = (f32[1,1,1024]{2,0,1:T(1,128)}, f32[1,1,1024]{2,0,1:T(1,128)S(1)}, u32[]{:S(2)}) copy-start(f32[1,1,1024]{2,0,1:T(1,128)S(1)} %get-tuple-element.173) | copy-start | bytes 12292
  70.5 153.4 %copy-start.47 = (f32[1,1,1024]{2,0,1:T(1,128)}, f32[1,1,1024]{2,0,1:T(1,128)S(1)}, u32[]{:S(2)}) copy-start(f32[1,1,1024]{2,0,1:T(1,128)S(1)} %get-tuple-element.176) | copy-start | bytes 12292
  70.5 153.4 %copy-start.48 = (f32[1,1,1024]{2,0,1:T(1,128)}, f32[1,1,1024]{2,0,1:T(1,128)S(1)}, u32[]{:S(2)}) copy-start(f32[1,1,1024]{2,0,1:T(1,128)S(1)} %get-tuple-element.177) | copy-start | bytes 12292
  70.5 153.4 %copy-start.49 = (f32[1,1,1024]{2,0,1:T(1,128)}, f32[1,1,1024]{2,0,1:T(1,128)S(1)}, u32[]{:S(2)}) copy-start(f32[1,1,1024]{2,0,1:T(1,128)S(1)} %get-tuple-element.178) | copy-start | bytes 12292
  70.5 153.4 %copy-start.60 = (f32[1,1,1024]{2,0,1:T(1,128)}, f32[1,1,1024]{2,0,1:T(1,128)S(1)}, u32[]{:S(2)}) copy-start(f32[1,1,1024]{2,0,1:T(1,128)S(1)} %get-tuple-element.166) | copy-start | bytes 12292
  70.6 197.2 %copy-start.54 = (f32[1,1,1024]{2,0,1:T(1,128)}, f32[1,1,1024]{2,0,1:T(1,128)S(1)}, u32[]{:S(2)}) copy-start(f32[1,1,1024]{2,0,1:T(1,128)S(1)} %get-tuple-element.175) | copy-start | bytes 12292
  70.6 197.2 %copy-start.57 = (f32[1,1,1024]{2,0,1:T(1,128)}, f32[1,1,1024]{2,0,1:T(1,128)S(1)}, u32[]{:S(2)}) copy-start(f32[1,1,1024]{2,0,1:T(1,128)S(1)} %get-tuple-element.165) | copy-start | bytes 12292
  70.6 204.9 %copy-start.52 = (f32[1,1,1024]{2,0,1:T(1,128)}, f32[1,1,1024]{2,0,1:T(1,128)S(1)}, u32[]{:S(2)}) copy-start(f32[1,1,1024]{2,0,1:T(1,128)S(1)} %get-tuple-element.171) | copy-start | bytes 12292
  70.6 206.0 %copy-start.50 = (f32[1,1,1024]{2,0,1:T(1,128)}, f32[1,1,1024]{2,0,1:T(1,128)S(1)}, u32[]{:S(2)}) copy-start(f32[1,1,1024]{2,0,1:T(1,128)S(1)} %get-tuple-element.172) | copy-start | bytes 12292
  80.5 31.1 %copy-start.29 = (bf16[2,128,1024]{2,1,0:T(8,128)(2,1)}, bf16[2,128,1024]{2,1,0:T(8,128)(2,1)S(1)}, u32[]{:S(2)}) copy-start(bf16[2,128,1024]{2,1,0:T(8,128)(2,1)S(1)} %collective-permute-done.5) | copy-start | bytes 1572868
  80.7 30.8 %copy-start.21 = (bf16[2,128,1024]{2,1,0:T(8,128)(2,1)}, bf16[2,128,1024]{2,1,0:T(8,128)(2,1)S(1)}, u32[]{:S(2)}) copy-start(bf16[2,128,1024]{2,1,0:T(8,128)(2,1)S(1)} %fusion.91) | copy-start | bytes 1572868
  80.7 15.9 %collective-permute-start.6 = (bf16[2,128,1024]{2,1,0:T(8,128)(2,1)S(1)}, bf16[2,128,1024]{2,1,0:T(8,128)(2,1)S(1)}, u32[]{:S(2)}, u32[]{:S(2)}) collective-permute-start(bf16[2,128,1024]{2,1,0:T(8,128)(2,1)S(1)} %fusion.91), channel_id=1, source_target_pairs={{0,16},{1,17},{2,18},{3,19},{4,20},{5,21},{6,22},{7,23},{8,24},{9,... | collective-permute-start | bytes 1572872 | tf_op jit(solution)/shard_map/ppermute | solution.py:10
  96.6 14.9 %copy-start.30 = (bf16[2,128,1024]{2,1,0:T(8,128)(2,1)}, bf16[2,128,1024]{2,1,0:T(8,128)(2,1)S(1)}, u32[]{:S(2)}) copy-start(bf16[2,128,1024]{2,1,0:T(8,128)(2,1)S(1)} %collective-permute-done.6) | copy-start | bytes 1572868
  96.9 14.7 %copy-start.22 = (bf16[2,128,1024]{2,1,0:T(8,128)(2,1)}, bf16[2,128,1024]{2,1,0:T(8,128)(2,1)S(1)}, u32[]{:S(2)}) copy-start(bf16[2,128,1024]{2,1,0:T(8,128)(2,1)S(1)} %fusion.98) | copy-start | bytes 1572868
  96.9 14.4 %collective-permute-start.7 = (bf16[2,128,1024]{2,1,0:T(8,128)(2,1)S(1)}, bf16[2,128,1024]{2,1,0:T(8,128)(2,1)S(1)}, u32[]{:S(2)}, u32[]{:S(2)}) collective-permute-start(bf16[2,128,1024]{2,1,0:T(8,128)(2,1)S(1)} %fusion.98), channel_id=1, source_target_pairs={{0,32},{1,33},{2,34},{3,35},{4,36},{5,37},{6,38},{7,39},{8,40},{9,... | collective-permute-start | bytes 1572872 | tf_op jit(solution)/shard_map/ppermute | solution.py:10
  124.1 22.8 %collective-permute-start.8 = (bf16[2,128,1024]{2,1,0:T(8,128)(2,1)S(1)}, bf16[2,128,1024]{2,1,0:T(8,128)(2,1)S(1)}, u32[]{:S(2)}, u32[]{:S(2)}) collective-permute-start(bf16[2,128,1024]{2,1,0:T(8,128)(2,1)S(1)} %get-tuple-element.185), channel_id=1, source_target_pairs={{32,0},{33,1},{34,2},{35,3},{36,4},{37,5},{38,6},{39,7},{40,8},{41... | collective-permute-start | bytes 1572872 | tf_op jit(solution)/shard_map/ppermute | solution.py:10
  147.0 34.4 %copy-start.27 = (bf16[2,128,1024]{2,1,0:T(8,128)(2,1)}, bf16[2,128,1024]{2,1,0:T(8,128)(2,1)S(1)}, u32[]{:S(2)}) copy-start(bf16[2,128,1024]{2,1,0:T(8,128)(2,1)S(1)} %collective-permute-done.8) | copy-start | bytes 1572868
  147.4 31.7 %collective-permute-start.9 = (bf16[2,128,1024]{2,1,0:T(8,128)(2,1)S(1)}, bf16[2,128,1024]{2,1,0:T(8,128)(2,1)S(1)}, u32[]{:S(2)}, u32[]{:S(2)}) collective-permute-start(bf16[2,128,1024]{2,1,0:T(8,128)(2,1)S(1)} %add_convert_fusion.18), channel_id=1, source_target_pairs={{16,0},{17,1},{18,2},{19,3},{20,4},{21,5},{22,6},{23,7},{24,8},{25... | collective-permute-start | bytes 1572872 | tf_op jit(solution)/shard_map/ppermute | solution.py:10
  181.4 42.5 %collective-permute-start.10 = (bf16[2,128,1024]{2,1,0:T(8,128)(2,1)}, bf16[2,128,1024]{2,1,0:T(8,128)(2,1)}, u32[]{:S(2)}, u32[]{:S(2)}) collective-permute-start(bf16[2,128,1024]{2,1,0:T(8,128)(2,1)} %add_convert_fusion.17), channel_id=1, source_target_pairs={{8,0},{9,1},{10,2},{11,3},{12,4},{13,5},{14,6},{15,7},{16,8},{17,9... | collective-permute-start | bytes 1572872 | tf_op jit(solution)/shard_map/ppermute | solution.py:10
  223.9 21.5 %copy-start.35 = (bf16[2,128,1024]{2,1,0:T(8,128)(2,1)S(1)}, bf16[2,128,1024]{2,1,0:T(8,128)(2,1)}, u32[]{:S(2)}) copy-start(bf16[2,128,1024]{2,1,0:T(8,128)(2,1)} %copy-done.33) | copy-start | bytes 1572868
  228.2 17.2 %copy-start.1 = (bf16[2,256,1024]{2,1,0:T(8,128)(2,1)S(1)}, bf16[2,256,1024]{2,1,0:T(8,128)(2,1)}, u32[]{:S(2)}) copy-start(bf16[2,256,1024]{2,1,0:T(8,128)(2,1)} %copy-done) | copy-start | bytes 3145732
  228.2 17.2 %copy-start.4 = (bf16[2,256,1024]{2,1,0:T(8,128)(2,1)S(1)}, bf16[2,256,1024]{2,1,0:T(8,128)(2,1)}, u32[]{:S(2)}) copy-start(bf16[2,256,1024]{2,1,0:T(8,128)(2,1)} %copy-done.3) | copy-start | bytes 3145732
  228.2 17.2 %copy-start.24 = (bf16[2,128,1024]{2,1,0:T(8,128)(2,1)S(1)}, bf16[2,128,1024]{2,1,0:T(8,128)(2,1)}, u32[]{:S(2)}) copy-start(bf16[2,128,1024]{2,1,0:T(8,128)(2,1)} %copy-done.23) | copy-start | bytes 1572868
  228.4 16.9 %collective-permute-start.11 = (bf16[2,128,1024]{2,1,0:T(8,128)(2,1)S(1)}, bf16[2,128,1024]{2,1,0:T(8,128)(2,1)S(1)}, u32[]{:S(2)}, u32[]{:S(2)}) collective-permute-start(bf16[2,128,1024]{2,1,0:T(8,128)(2,1)S(1)} %add_convert_fusion.16), channel_id=1, source_target_pairs={{4,0},{5,1},{6,2},{7,3},{8,4},{9,5},{10,6},{11,7},{12,8},{13,9},{1... | collective-permute-start | bytes 1572872 | tf_op jit(solution)/shard_map/ppermute | solution.py:10
  247.8 18.8 %copy-start.14 = (bf16[2,256,1024]{2,1,0:T(8,128)(2,1)S(1)}, bf16[2,256,1024]{2,1,0:T(8,128)(2,1)}, u32[]{:S(2)}) copy-start(bf16[2,256,1024]{2,1,0:T(8,128)(2,1)} %copy-done.13) | copy-start | bytes 3145732
  247.8 18.8 %copy-start.26 = (bf16[2,128,1024]{2,1,0:T(8,128)(2,1)S(1)}, bf16[2,128,1024]{2,1,0:T(8,128)(2,1)}, u32[]{:S(2)}) copy-start(bf16[2,128,1024]{2,1,0:T(8,128)(2,1)} %copy-done.25) | copy-start | bytes 1572868
  248.1 19.7 %copy-start.9 = (bf16[2,256,1024]{2,1,0:T(8,128)(2,1)S(1)}, bf16[2,256,1024]{2,1,0:T(8,128)(2,1)}, u32[]{:S(2)}) copy-start(bf16[2,256,1024]{2,1,0:T(8,128)(2,1)} %copy-done.8) | copy-start | bytes 3145732
  248.1 19.7 %copy-start.11 = (bf16[1,2,128,1024]{3,2,1,0:T(8,128)(2,1)S(1)}, bf16[1,2,128,1024]{3,2,1,0:T(8,128)(2,1)}, u32[]{:S(2)}) copy-start(bf16[1,2,128,1024]{3,2,1,0:T(8,128)(2,1)} %param.5) | copy-start | bytes 1572868
  248.1 19.7 %copy-start.38 = (bf16[2,128,1024]{2,1,0:T(8,128)(2,1)S(1)}, bf16[2,128,1024]{2,1,0:T(8,128)(2,1)}, u32[]{:S(2)}) copy-start(bf16[2,128,1024]{2,1,0:T(8,128)(2,1)} %copy-done.37) | copy-start | bytes 1572868
  248.1 18.6 %collective-permute-start.12 = (bf16[2,128,1024]{2,1,0:T(8,128)(2,1)S(1)}, bf16[2,128,1024]{2,1,0:T(8,128)(2,1)S(1)}, u32[]{:S(2)}, u32[]{:S(2)}) collective-permute-start(bf16[2,128,1024]{2,1,0:T(8,128)(2,1)S(1)} %add_convert_fusion.15), channel_id=1, source_target_pairs={{2,0},{3,1},{4,2},{5,3},{6,4},{7,5},{8,6},{9,7},{10,8},{11,9},{12,... | collective-permute-start | bytes 1572872 | tf_op jit(solution)/shard_map/ppermute | solution.py:10
  267.8 6.2 %copy-start.7 = (bf16[2,256,1024]{2,1,0:T(8,128)(2,1)S(1)}, bf16[2,256,1024]{2,1,0:T(8,128)(2,1)}, u32[]{:S(2)}) copy-start(bf16[2,256,1024]{2,1,0:T(8,128)(2,1)} %copy-done.6) | copy-start | bytes 3145732
  270.1 3.9 %collective-permute-start.13 = (bf16[2,128,1024]{2,1,0:T(8,128)(2,1)S(1)}, bf16[2,128,1024]{2,1,0:T(8,128)(2,1)S(1)}, u32[]{:S(2)}, u32[]{:S(2)}) collective-permute-start(bf16[2,128,1024]{2,1,0:T(8,128)(2,1)S(1)} %get-tuple-element.148), channel_id=1, source_target_pairs={{1,0},{2,1},{3,2},{4,3},{5,4},{6,5},{7,6},{8,7},{9,8},{10,9},{11,1... | collective-permute-start | bytes 1572872 | tf_op jit(solution)/shard_map/ppermute | solution.py:10
  287.4 10.3 %copy-start.5 = (bf16[2,256,1024]{2,1,0:T(8,128)(2,1)S(1)}, bf16[2,256,1024]{2,1,0:T(8,128)(2,1)}, u32[]{:S(2)}) copy-start(bf16[2,256,1024]{2,1,0:T(8,128)(2,1)} %copy-done.3) | copy-start | bytes 3145732
  287.4 10.3 %copy-start.16 = (f32[2,128,1024]{2,1,0:T(8,128)S(1)}, f32[2,128,1024]{2,1,0:T(8,128)}, u32[]{:S(2)}) copy-start(f32[2,128,1024]{2,1,0:T(8,128)} %copy-done.15) | copy-start | bytes 3145732
  287.5 10.3 %copy-start.18 = (f32[2,128,1024]{2,1,0:T(8,128)S(1)}, f32[2,128,1024]{2,1,0:T(8,128)}, u32[]{:S(2)}) copy-start(f32[2,128,1024]{2,1,0:T(8,128)} %copy-done.17) | copy-start | bytes 3145732
  287.5 10.3 %collective-permute-start.14 = (bf16[2,127,1024]{2,1,0:T(8,128)(2,1)}, bf16[2,127,1024]{2,1,0:T(8,128)(2,1)S(1)}, u32[]{:S(2)}, u32[]{:S(2)}) collective-permute-start(bf16[2,127,1024]{2,1,0:T(8,128)(2,1)} %concatenate.46), channel_id=1, source_target_pairs={{1,0},{2,1},{3,2},{4,3},{5,4},{6,5},{7,6},{8,7},{9,8},{10,9},{11,1... | collective-permute-start | bytes 1560584 | tf_op jit(solution)/shard_map/ppermute | solution.py:10
  297.7 6.5 %copy-start.40 = (bf16[2,127,1024]{2,1,0:T(8,128)(2,1)}, bf16[2,127,1024]{2,1,0:T(8,128)(2,1)S(1)}, u32[]{:S(2)}) copy-start(bf16[2,127,1024]{2,1,0:T(8,128)(2,1)S(1)} %collective-permute-done.14) | copy-start | bytes 1560580
  305.0 36.4 %copy-start.59 = (f32[1,1,1024]{2,0,1:T(1,128)S(1)}, f32[1,1,1024]{2,0,1:T(1,128)}, u32[]{:S(2)}) copy-start(f32[1,1,1024]{2,0,1:T(1,128)} %copy-done.57) | copy-start | bytes 12292
  306.2 19.8 %collective-permute-start.15 = (f32[16,1024]{1,0:T(8,128)S(1)}, f32[16,1024]{1,0:T(8,128)S(1)}, u32[]{:S(2)}, u32[]{:S(2)}) collective-permute-start(f32[16,1024]{1,0:T(8,128)S(1)} %concatenate.54), channel_id=1, source_target_pairs={{0,1},{1,0},{2,3},{3,2},{4,5},{5,4},{6,7},{7,6},{8,9},{9,8},{10,11... | collective-permute-start | bytes 196616 | tf_op jit(solution)/shard_map/ppermute | solution.py:34
  326.0 4.4 %collective-permute-start.16 = (f32[16,1024]{1,0:T(8,128)S(1)}, f32[16,1024]{1,0:T(8,128)S(1)}, u32[]{:S(2)}, u32[]{:S(2)}) collective-permute-start(f32[16,1024]{1,0:T(8,128)S(1)} %add.1028), channel_id=1, source_target_pairs={{0,2},{1,3},{2,0},{3,1},{4,6},{5,7},{6,4},{7,5},{8,10},{9,11},{10,... | collective-permute-start | bytes 196616 | tf_op jit(solution)/shard_map/ppermute | solution.py:34
  330.4 6.1 %collective-permute-start.17 = (f32[16,1024]{1,0:T(8,128)S(1)}, f32[16,1024]{1,0:T(8,128)S(1)}, u32[]{:S(2)}, u32[]{:S(2)}) collective-permute-start(f32[16,1024]{1,0:T(8,128)S(1)} %add.1029), channel_id=1, source_target_pairs={{0,4},{1,5},{2,6},{3,7},{4,0},{5,1},{6,2},{7,3},{8,12},{9,13},{10,... | collective-permute-start | bytes 196616 | tf_op jit(solution)/shard_map/ppermute | solution.py:34
  336.6 4.4 %collective-permute-start.18 = (f32[16,1024]{1,0:T(8,128)S(1)}, f32[16,1024]{1,0:T(8,128)S(1)}, u32[]{:S(2)}, u32[]{:S(2)}) collective-permute-start(f32[16,1024]{1,0:T(8,128)S(1)} %add.1030), channel_id=1, source_target_pairs={{0,8},{1,9},{2,10},{3,11},{4,12},{5,13},{6,14},{7,15},{8,0},{9,1},... | collective-permute-start | bytes 196616 | tf_op jit(solution)/shard_map/ppermute | solution.py:34
  340.9 5.3 %collective-permute-start.19 = (f32[16,1024]{1,0:T(8,128)S(1)}, f32[16,1024]{1,0:T(8,128)S(1)}, u32[]{:S(2)}, u32[]{:S(2)}) collective-permute-start(f32[16,1024]{1,0:T(8,128)S(1)} %add.1031), channel_id=1, source_target_pairs={{0,16},{1,17},{2,18},{3,19},{4,20},{5,21},{6,22},{7,23},{8,24},{9,... | collective-permute-start | bytes 196616 | tf_op jit(solution)/shard_map/ppermute | solution.py:34
  346.2 8.4 %collective-permute-start.20 = (f32[16,1024]{1,0:T(8,128)S(1)}, f32[16,1024]{1,0:T(8,128)S(1)}, u32[]{:S(2)}, u32[]{:S(2)}) collective-permute-start(f32[16,1024]{1,0:T(8,128)S(1)} %add.1032), channel_id=1, source_target_pairs={{0,32},{1,33},{2,34},{3,35},{4,36},{5,37},{6,38},{7,39},{8,40},{9,... | collective-permute-start | bytes 196616 | tf_op jit(solution)/shard_map/ppermute | solution.py:34
  (59 other events, 182.6 us)
Sparse Core Ops, SparseCore 0:
  187.3 186.0 reduce-scatter.1
